TPU v7x, 256 devices: a whole 4x4x8 slice. The times are simulated.
256 devices in a mesh: dp: 64 (over x, z, core), pipe: 4 (over y).
Axes of the slice: x: 4, y: 4, z: 8, core: 2. Of those that a mesh axis runs over, the one named last changes fastest.
Arguments:
- tokens: bfloat16 [8192, 2560], P('dp'), may hold values from -6 to 6
- norm_gains: bfloat16 [4, 2560], P('pipe', 'dp'), may hold values from 0.099609375 to 1.8984375
- up_weights: bfloat16 [4, 64, 128, 128], P('pipe', 'dp'), may hold values from -0.5 to 0.5
- down_weights: bfloat16 [4, 64, 128, 128], P('pipe', 'dp'), may hold values from -0.3125 to 0.3125
- coords: int32 [4, 4, 64], P('pipe'), may hold values from 0 to 79, as said below
- cotangent: bfloat16 [8192, 2560], P('dp'), may hold values from -6 to 6
Outputs:
- grad_up: float32 [4, 64, 128, 128], P('pipe', 'dp')
- grad_down: float32 [4, 64, 128, 128], P('pipe', 'dp')
- grad_gain: float32 [4, 2560], P('pipe', 'dp')
- grad_inputs: bfloat16 [4, 8192, 2560], P('pipe', 'dp')
Inputs may be any that keep to these rules, and one draw needn't show every extreme that they name: For every layer the 64 pairs (coords[l,0,b], coords[l,1,b]) are distinct, and so are the pairs (coords[l,2,b], coords[l,3,b]); rows 0 and 3 lie below 20, rows 1 and 2 below 80.
All inputs are finite; a program needn't handle non-finite values.
Results may differ from a plain program's by a relative error of at most 0.011.
Values may be sent and summed in bfloat16 or wider, within the bound.
No kernel may reach another device: no remote copies, remote signals or barrier semaphores. Data moves between devices by JAX's collectives and lax.ppermute only.
A program may use at most 128 MiB of HBM per device.

v0:
```python
import math
import jax
import jax.numpy as jnp
from jax import lax
from jax.sharding import PartitionSpec as P

FF = 10240
MICRO = 2
epsilon = 1e-05


def from_behind(value, axis, by):
    size = lax.axis_size(axis)
    pairs = [(i, i + by) for i in range(size) if 0 <= i + by < size]
    return lax.ppermute(value, axis, pairs)


def norm_parts(inputs, gain_row):
    widened = inputs.astype(jnp.float32)
    inverse = lax.rsqrt(jnp.mean(widened * widened, axis=-1, keepdims=True) + epsilon)
    unit_rows = widened * inverse
    normed = (unit_rows * gain_row.astype(jnp.float32)).astype(jnp.bfloat16)
    return (widened, inverse, unit_rows, normed)


def to_panels(values, panel_width):
    row_count = values.shape[0]
    return jnp.transpose(values.reshape(row_count, -1, panel_width), (1, 0, 2))


def from_panels(panels):
    return jnp.transpose(panels, (1, 0, 2)).reshape(
        panels.shape[1], panels.shape[0] * panels.shape[2]
    )


def panel_product(panels, blocks, pick_index, put_index, put_count, form):
    picked = jnp.take(panels, pick_index, axis=0)
    products = jnp.einsum(form, picked, blocks, preferred_element_type=jnp.float32)
    placing = (put_index[:, None] == jnp.arange(put_count, dtype=jnp.int32)[None, :]).astype(
        jnp.float32
    )
    return jnp.einsum("brc,bp->prc", products, placing, precision=lax.Precision.HIGH)


def up_product(inputs, gain_row, up_blocks, block_links, hidden_panels, panel_width):
    normed = norm_parts(inputs, gain_row)[3]
    return panel_product(
        to_panels(normed, panel_width),
        up_blocks,
        block_links[0],
        block_links[1],
        hidden_panels,
        "bri,bio->bro",
    )


def layer_forward(
    inputs, gain_row, up_blocks, down_blocks, block_links, hidden_panels, model_panels, panel_width
):
    widened, inverse, unit_rows, normed = norm_parts(inputs, gain_row)
    before = panel_product(
        to_panels(normed, panel_width),
        up_blocks,
        block_links[0],
        block_links[1],
        hidden_panels,
        "bri,bio->bro",
    )
    active = jax.nn.gelu(before).astype(jnp.bfloat16)
    added = from_panels(
        panel_product(
            active, down_blocks, block_links[2], block_links[3], model_panels, "bri,bio->bro"
        )
    )
    return ((widened + added).astype(jnp.bfloat16), before)


def layer_backward(
    inputs,
    upstream,
    before,
    gain_row,
    up_blocks,
    down_blocks,
    block_links,
    hidden_panels,
    model_panels,
    panel_width,
):
    widened, inverse, unit_rows, normed = norm_parts(inputs, gain_row)
    upstream_panels = to_panels(upstream, panel_width)
    active_full, gelu_slope = jax.jvp(jax.nn.gelu, (before,), (jnp.ones_like(before),))
    active = active_full.astype(jnp.bfloat16)
    grad_active = panel_product(
        upstream_panels, down_blocks, block_links[3], block_links[2], hidden_panels, "bro,bio->bri"
    )
    grad_before = (grad_active * gelu_slope).astype(jnp.bfloat16)
    grad_normed = from_panels(
        panel_product(
            grad_before, up_blocks, block_links[1], block_links[0], model_panels, "bro,bio->bri"
        )
    )
    gain_grad = jnp.sum(grad_normed * unit_rows, axis=0)
    grad_unit = grad_normed * gain_row.astype(jnp.float32)
    centered = grad_unit - unit_rows * jnp.mean(grad_unit * unit_rows, axis=-1, keepdims=True)
    grad_local = (upstream.astype(jnp.float32) + inverse * centered).astype(jnp.bfloat16)
    return (
        grad_local,
        gain_grad,
        to_panels(normed, panel_width),
        active,
        grad_before,
        upstream_panels,
    )


def own_slots(collected, first):
    stacked = jnp.stack(collected)
    return lax.dynamic_slice_in_dim(stacked, first, MICRO, 0)


def shards(tokens, norm_gains, up_weights, down_weights, coords, cotangent):
    phases = lax.axis_size("pipe")
    section = lax.axis_index("pipe")
    panel_width = up_weights.shape[2]
    model_width = tokens.shape[1]
    token_rows = tokens.shape[0]
    hidden_panels = FF // panel_width
    model_panels = model_width // panel_width
    group_rows = token_rows // MICRO
    block_links = coords[0]
    block_width = panel_width * panel_width
    gain_count = norm_gains.shape[1]
    gain_room = -(-gain_count // 128) * 128
    packed = jnp.concatenate(
        [
            up_weights.reshape(1, 1, block_width),
            down_weights.reshape(1, 1, block_width),
            jnp.pad(
                norm_gains.reshape(1, 1, gain_count), ((0, 0), (0, 0), (0, gain_room - gain_count))
            ),
        ],
        axis=2,
    )
    gathered = lax.all_gather(packed, "dp", axis=1, tiled=True)[0]
    block_count = gathered.shape[0]
    up_blocks = gathered[:, :block_width].reshape(block_count, panel_width, panel_width)
    down_blocks = gathered[:, block_width : 2 * block_width].reshape(
        block_count, panel_width, panel_width
    )
    gain_row = gathered[:, 2 * block_width : 2 * block_width + gain_count].reshape(-1)
    token_groups = tokens.reshape(MICRO, group_rows, model_width)
    cot_groups = cot_groups_of = cotangent.reshape(MICRO, group_rows, model_width)
    last_tick = MICRO + phases - 2
    input_list = []
    before_list = []
    arriving = jnp.zeros((group_rows, model_width), jnp.bfloat16)
    for moment in range(last_tick + 1):
        current = jnp.where(section == 0, token_groups[min(moment, MICRO - 1)], arriving)
        input_list.append(current)
        leaving, before = layer_forward(
            current,
            gain_row,
            up_blocks,
            down_blocks,
            block_links,
            hidden_panels,
            model_panels,
            panel_width,
        )
        before_list.append(before)
        if moment < last_tick:
            arriving = from_behind(leaving, "pipe", 1)
    input_stack = jnp.stack(input_list)
    before_stack = jnp.stack(before_list)
    gain_total = jnp.zeros((model_width,), jnp.float32)
    grad_list = []
    normed_list = []
    upper_list = []
    active_list = []
    slope_list = []
    arriving = jnp.zeros((group_rows, model_width), jnp.bfloat16)
    for moment in range(last_tick + 1):
        slot_index = moment - (phases - 1 - section)
        slot_live = (slot_index >= 0) & (slot_index < MICRO)
        tick_place = jnp.clip(slot_index, 0, MICRO - 1) + section
        upstream = jnp.where(section == phases - 1, cot_groups_of[min(moment, MICRO - 1)], arriving)
        inputs = lax.dynamic_index_in_dim(input_stack, tick_place, 0, keepdims=False)
        before = lax.dynamic_index_in_dim(before_stack, tick_place, 0, keepdims=False)
        grad_local, gain_grad, normed, active, grad_before, upper = layer_backward(
            inputs,
            upstream,
            before,
            gain_row,
            up_blocks,
            down_blocks,
            block_links,
            hidden_panels,
            model_panels,
            panel_width,
        )
        gain_total = gain_total + jnp.where(slot_live, gain_grad, 0.0)
        grad_list.append(grad_local)
        normed_list.append(normed)
        upper_list.append(upper)
        active_list.append(active)
        slope_list.append(grad_before)
        if moment < last_tick:
            arriving = from_behind(grad_local, "pipe", -1)
    first = phases - 1 - section
    grad_store = own_slots(grad_list, first)
    normed_all = own_slots(normed_list, first)
    upper_all = own_slots(upper_list, first)
    active_all = own_slots(active_list, first)
    slope_all = own_slots(slope_list, first)
    grad_scale = 1.0 / math.sqrt(token_rows * lax.axis_size("dp"))
    up_total = jnp.einsum(
        "mbri,mbro->bio",
        jnp.take(normed_all, block_links[0], axis=1),
        jnp.take(slope_all, block_links[1], axis=1),
        preferred_element_type=jnp.float32,
    )
    down_total = jnp.einsum(
        "mbri,mbro->bio",
        jnp.take(active_all, block_links[2], axis=1),
        jnp.take(upper_all, block_links[3], axis=1),
        preferred_element_type=jnp.float32,
    )
    gain_parts = jnp.pad(
        gain_total.reshape(block_count, gain_count), ((0, 0), (0, 8 * 128 - gain_count))
    )
    totals = jnp.concatenate(
        [
            up_total.reshape(block_count, block_width),
            down_total.reshape(block_count, block_width),
            gain_parts,
        ],
        axis=1,
    )
    summed = (
        lax.psum_scatter(
            totals.reshape(1, block_count, -1, 128), "dp", scatter_dimension=1, tiled=True
        ).reshape(-1)
        * grad_scale
    )
    up_out = summed[:block_width].reshape(1, 1, panel_width, panel_width)
    down_out = summed[block_width : 2 * block_width].reshape(1, 1, panel_width, panel_width)
    gain_out = summed[2 * block_width : 2 * block_width + gain_count].reshape(1, gain_count)
    return (up_out, down_out, gain_out, grad_store.reshape(1, token_rows, model_width))


def solution(mesh):
    in_specs = (
        P("dp", None),
        P("pipe", "dp"),
        P("pipe", "dp", None, None),
        P("pipe", "dp", None, None),
        P("pipe", None, None),
        P("dp", None),
    )
    out_specs = (
        P("pipe", "dp", None, None),
        P("pipe", "dp", None, None),
        P("pipe", "dp"),
        P("pipe", "dp", None),
    )
    return jax.shard_map(shards, mesh=mesh, in_specs=in_specs, out_specs=out_specs, check_vma=False)
```

profile of v0, /device:TPU:8, one launch (start us, length us, event | category | flops | bytes accessed | tf_op | source)
XLA Modules:
  0.0 626.4 jit_solution(7334065427860682173)
XLA Ops:
  12.9 84.3 %all-gather.2.cloned.1.call-done = bf16[1,64,32896]{2,0,1:T(2,128)(2,1)} async-done(((bf16[1,1,32896]{2,0,1:T(2,128)(2,1)}), bf16[1,64,32896]{2,0,1:T(2,128)(2,1)}) %all-gather.2.cloned.1.call-update) | async-done | bytes 4210704 | tf_op jit(solution)/shard_map/all_gather | solution.py:146
  97.2 3.8 copy.258
  129.0 7.3 %collective-permute-done = bf16[64,2560]{1,0:T(8,128)(2,1)S(1)} collective-permute-done((bf16[64,2560]{1,0:T(8,128)(2,1)S(1)}, bf16[64,2560]{1,0:T(8,128)(2,1)S(1)}, u32[]{:S(2)}, u32[]{:S(2)}) %collective-permute-start) | collective-permute-done | bytes 327712 | tf_op jit(solution)/shard_map/ppermute | solution.py:15
  159.6 6.8 %collective-permute-done.1 = bf16[64,2560]{1,0:T(8,128)(2,1)} collective-permute-done((bf16[64,2560]{1,0:T(8,128)(2,1)}, bf16[64,2560]{1,0:T(8,128)(2,1)}, u32[]{:S(2)}, u32[]{:S(2)}) %collective-permute-start.1) | collective-permute-done | bytes 327712 | tf_op jit(solution)/shard_map/ppermute | solution.py:15
  188.3 3.6 collective-permute-start.2
  219.8 3.9 collective-permute-start.3
  233.7 3.6 bitcast_dynamic-update-slice_fusion
  237.3 3.8 fusion.201
  241.2 6.7 %bitcast_dynamic-update-slice_fusion.9 = (bf16[5,80,64,128]{3,1,2,0:T(8,128)(2,1)}, bf16[80,64,128]{2,0,1:T(8,128)(2,1)S(1)}) fusion(f32[5,80,64,128]{3,1,2,0:T(8,128)} %bitcast_dynamic-update-slice_fusion, s32[]{:T(128)S(6)} %select_n.163, f32[64,64,128]{2,1,0:T(8,128)S(1)} %copy-done.25, s32[64]{0:T(128)S(1)} %get-tuple-element.59), kind=kOutput, calls=%fused_computation.248 | convolution fusion | flops 263459840 | bytes 7340292 | tf_op jit(solution)/shard_map/brc,bp->prc/dot_general | solution.py:43
  281.1 3.7 fusion.200
  284.8 3.7 fusion.199
  288.5 3.8 fusion.198
  294.1 3.7 fusion.197
  308.6 6.9 %bitcast_dynamic-update-slice_fusion.8 = (bf16[5,80,64,128]{3,1,2,0:T(8,128)(2,1)}, bf16[80,64,128]{2,0,1:T(8,128)(2,1)S(1)}) fusion(bf16[5,80,64,128]{3,1,2,0:T(8,128)(2,1)} %get-tuple-element.79, f32[5,80,64,128]{3,1,2,0:T(8,128)} %bitcast_dynamic-update-slice_fusion, s32[]{:T(128)S(6)} %select_n.164, f32[64,64,128]{2,1,0:T(8,128)S(1)} %fusion.216, ...), kind=kOutput, calls=%fused_computation.247 | convolution fusion | flops 263459840 | bytes 7340292 | tf_op jit(solution)/shard_map/brc,bp->prc/dot_general | solution.py:43
  345.5 6.9 %bitcast_dynamic-update-slice_fusion.7 = (bf16[5,80,64,128]{3,1,2,0:T(8,128)(2,1)}, bf16[80,64,128]{2,0,1:T(8,128)(2,1)S(1)}) fusion(bf16[5,80,64,128]{3,1,2,0:T(8,128)(2,1)} %get-tuple-element.81, f32[5,80,64,128]{3,1,2,0:T(8,128)} %bitcast_dynamic-update-slice_fusion, s32[]{:T(128)S(6)} %select_n.165, f32[64,64,128]{2,1,0:T(8,128)S(1)} %fusion.212, ...), kind=kOutput, calls=%fused_computation.246 | convolution fusion | flops 263459840 | bytes 7340292 | tf_op jit(solution)/shard_map/brc,bp->prc/dot_general | solution.py:43
  369.8 3.9 copy.116
  373.7 4.0 gather_fusion.20
  385.8 7.1 %bitcast_dynamic-update-slice_fusion.6 = (bf16[5,80,64,128]{3,1,2,0:T(8,128)(2,1)}, bf16[80,64,128]{2,0,1:T(8,128)(2,1)S(1)}) fusion(bf16[5,80,64,128]{3,1,2,0:T(8,128)(2,1)} %get-tuple-element.83, f32[5,80,64,128]{3,1,2,0:T(8,128)} %bitcast_dynamic-update-slice_fusion, s32[]{:T(128)S(6)} %select_n.166, f32[64,64,128]{2,1,0:T(8,128)S(1)} %fusion.208, ...), kind=kOutput, calls=%fused_computation.245 | convolution fusion | flops 263459840 | bytes 7340292 | tf_op jit(solution)/shard_map/brc,bp->prc/dot_general | solution.py:43
  419.7 6.8 %bitcast_dynamic-update-slice_fusion.5 = (bf16[5,80,64,128]{3,1,2,0:T(8,128)(2,1)}, bf16[80,64,128]{2,0,1:T(8,128)(2,1)S(1)}) fusion(bf16[5,80,64,128]{3,1,2,0:T(8,128)(2,1)} %get-tuple-element.85, f32[5,80,64,128]{3,1,2,0:T(8,128)} %bitcast_dynamic-update-slice_fusion, s32[]{:T(128)S(6)} %select_n.167, f32[64,64,128]{2,1,0:T(8,128)S(1)} %fusion.204, ...), kind=kOutput, calls=%fused_computation.244 | convolution fusion | flops 263459840 | bytes 7340292 | tf_op jit(solution)/shard_map/brc,bp->prc/dot_general | solution.py:43
  444.4 4.4 copy.260
  454.0 4.6 copy.259
  458.8 3.8 fusion
  462.5 4.9 copy.145
  471.4 145.8 %reduce-scatter.5.cloned.1.call-done = f32[1,1,264,128]{3,2,1,0:T(8,128)} async-done(((f32[1,64,264,128]{3,2,1,0:T(8,128)}), f32[1,1,264,128]{3,2,1,0:T(8,128)}) %reduce-scatter.5.cloned.1.call-update) | async-done | bytes 135184
  (301 shorter events, 273.3 us)
Async XLA Ops:
  7.2 90.0 %all-gather.2.cloned.1.call-start = ((), (), s32[]{:S(2)}) async-start(), calls=%async_computation.1 | async-start | bytes 8552960 | tf_op jit(solution)/shard_map/all_gather | solution.py:146
  10.3 606.9 %reduce-scatter.5.cloned.1.call-start = ((), (), s32[]{:S(2)}) async-start(), calls=%async_computation.2 | async-start | bytes 8785920
  12.0 203.4 %copy-start.42 = (pred[64]{0:T(512)(128)(4,1)}, pred[64]{0:T(512)(128)(4,1)S(1)}, u32[]{:S(2)}) copy-start(pred[64]{0:T(512)(128)(4,1)S(1)} %get-tuple-element.60) | copy-start | bytes 196
  12.0 219.7 %copy-start.37 = (pred[64]{0:T(512)(128)(4,1)}, pred[64]{0:T(512)(128)(4,1)S(1)}, u32[]{:S(2)}) copy-start(pred[64]{0:T(512)(128)(4,1)S(1)} %get-tuple-element.62) | copy-start | bytes 196
  12.1 200.4 %copy-start.47 = (s32[1024]{0:T(1024)}, s32[1024]{0:T(1024)S(1)}, u32[]{:S(2)}) copy-start(s32[1024]{0:T(1024)S(1)} %get-tuple-element.91) | copy-start | bytes 12292
  12.1 218.0 %copy-start.44 = (s32[1024]{0:T(1024)}, s32[1024]{0:T(1024)S(1)}, u32[]{:S(2)}) copy-start(s32[1024]{0:T(1024)S(1)} %get-tuple-element.92) | copy-start | bytes 12292
  12.9 228.3 %copy-start.58 = (s32[64]{0:T(128)}, s32[64]{0:T(128)S(1)}, u32[]{:S(2)}) copy-start(s32[64]{0:T(128)S(1)} %get-tuple-element.59) | copy-start | bytes 772
  124.6 11.8 %collective-permute-start = (bf16[64,2560]{1,0:T(8,128)(2,1)S(1)}, bf16[64,2560]{1,0:T(8,128)(2,1)S(1)}, u32[]{:S(2)}, u32[]{:S(2)}) collective-permute-start(bf16[64,2560]{1,0:T(8,128)(2,1)S(1)} %fusion.309), channel_id=1, source_target_pairs={{0,1},{1,2},{2,3},{4,5},{5,6},{6,7},{8,9},{9,10},{10,11},{12,13},{... | collective-permute-start | bytes 983048 | tf_op jit(solution)/shard_map/ppermute | solution.py:15
  129.0 100.9 %copy-start.26 = (f32[2560]{0:T(1024)}, f32[2560]{0:T(1024)S(1)}, u32[]{:S(2)}) copy-start(f32[2560]{0:T(1024)S(1)} %reshape.565) | copy-start | bytes 30724
  152.6 6.1 copy-start.1
  155.1 11.3 %collective-permute-start.1 = (bf16[64,2560]{1,0:T(8,128)(2,1)}, bf16[64,2560]{1,0:T(8,128)(2,1)}, u32[]{:S(2)}, u32[]{:S(2)}) collective-permute-start(bf16[64,2560]{1,0:T(8,128)(2,1)} %fusion.282), channel_id=1, source_target_pairs={{0,1},{1,2},{2,3},{4,5},{5,6},{6,7},{8,9},{9,10},{10,11},{12,13},{... | collective-permute-start | bytes 983048 | tf_op jit(solution)/shard_map/ppermute | solution.py:15
  188.3 10.3 %collective-permute-start.2 = (bf16[64,2560]{1,0:T(8,128)(2,1)}, bf16[64,2560]{1,0:T(8,128)(2,1)}, u32[]{:S(2)}, u32[]{:S(2)}) collective-permute-start(bf16[64,2560]{1,0:T(8,128)(2,1)} %fusion.286), channel_id=1, source_target_pairs={{0,1},{1,2},{2,3},{4,5},{5,6},{6,7},{8,9},{9,10},{10,11},{12,13},{... | collective-permute-start | bytes 983048 | tf_op jit(solution)/shard_map/ppermute | solution.py:15
  192.5 12.1 %copy-start.45 = (s32[1024]{0:T(1024)}, s32[1024]{0:T(1024)S(1)}, u32[]{:S(2)}) copy-start(s32[1024]{0:T(1024)S(1)} %get-tuple-element.90) | copy-start | bytes 12292
  219.8 9.1 %collective-permute-start.3 = (bf16[64,2560]{1,0:T(8,128)(2,1)S(1)}, bf16[64,2560]{1,0:T(8,128)(2,1)S(1)}, u32[]{:S(2)}, u32[]{:S(2)}) collective-permute-start(bf16[64,2560]{1,0:T(8,128)(2,1)S(1)} %fusion.290), channel_id=1, source_target_pairs={{0,1},{1,2},{2,3},{4,5},{5,6},{6,7},{8,9},{9,10},{10,11},{12,13},{... | collective-permute-start | bytes 983048 | tf_op jit(solution)/shard_map/ppermute | solution.py:15
  264.9 6.2 copy-start.28
  264.9 6.2 copy-start.50
  267.7 32.8 %collective-permute-start.4 = (bf16[64,2560]{1,0:T(8,128)(2,1)}, bf16[64,2560]{1,0:T(8,128)(2,1)}, u32[]{:S(2)}, u32[]{:S(2)}) collective-permute-start(bf16[64,2560]{1,0:T(8,128)(2,1)} %fusion.276), channel_id=1, source_target_pairs={{1,0},{2,1},{3,2},{5,4},{6,5},{7,6},{9,8},{10,9},{11,10},{13,12},{... | collective-permute-start | bytes 983048 | tf_op jit(solution)/shard_map/ppermute | solution.py:15
  278.1 15.1 %copy-start.9 = (f32[64,20,128]{2,1,0:T(8,128)}, f32[64,20,128]{2,1,0:T(8,128)S(1)}, u32[]{:S(2)}) copy-start(f32[64,20,128]{2,1,0:T(8,128)S(1)} %reshape.570) | copy-start | bytes 1966084
  278.7 14.5 %copy-start.53 = (f32[64]{0:T(128)}, f32[64]{0:T(128)S(1)}, u32[]{:S(2)}) copy-start(f32[64]{0:T(128)S(1)} %add_rsqrt_fusion.3) | copy-start | bytes 772
  299.0 9.6 %copy-start.7 = (f32[64,20,128]{2,1,0:T(8,128)}, f32[64,20,128]{2,1,0:T(8,128)S(1)}, u32[]{:S(2)}) copy-start(f32[64,20,128]{2,1,0:T(8,128)S(1)} %reshape.572) | copy-start | bytes 1966084
  328.0 9.5 %collective-permute-start.5 = (bf16[64,2560]{1,0:T(8,128)(2,1)}, bf16[64,2560]{1,0:T(8,128)(2,1)}, u32[]{:S(2)}, u32[]{:S(2)}) collective-permute-start(bf16[64,2560]{1,0:T(8,128)(2,1)} %get-tuple-element.28), channel_id=1, source_target_pairs={{1,0},{2,1},{3,2},{5,4},{6,5},{7,6},{9,8},{10,9},{11,10},{13,12},{... | collective-permute-start | bytes 983048 | tf_op jit(solution)/shard_map/ppermute | solution.py:15
  334.5 11.0 %copy-start.5 = (f32[64,20,128]{2,1,0:T(8,128)}, f32[64,20,128]{2,1,0:T(8,128)S(1)}, u32[]{:S(2)}) copy-start(f32[64,20,128]{2,1,0:T(8,128)S(1)} %reshape.574) | copy-start | bytes 1966084
  364.2 15.3 %collective-permute-start.6 = (bf16[64,2560]{1,0:T(8,128)(2,1)}, bf16[64,2560]{1,0:T(8,128)(2,1)}, u32[]{:S(2)}, u32[]{:S(2)}) collective-permute-start(bf16[64,2560]{1,0:T(8,128)(2,1)} %get-tuple-element.26), channel_id=1, source_target_pairs={{1,0},{2,1},{3,2},{5,4},{6,5},{7,6},{9,8},{10,9},{11,10},{13,12},{... | collective-permute-start | bytes 983048 | tf_op jit(solution)/shard_map/ppermute | solution.py:15
  404.6 9.0 %collective-permute-start.7 = (bf16[64,2560]{1,0:T(8,128)(2,1)S(1)}, bf16[64,2560]{1,0:T(8,128)(2,1)S(1)}, u32[]{:S(2)}, u32[]{:S(2)}) collective-permute-start(bf16[64,2560]{1,0:T(8,128)(2,1)S(1)} %get-tuple-element.24), channel_id=1, source_target_pairs={{1,0},{2,1},{3,2},{5,4},{6,5},{7,6},{9,8},{10,9},{11,10},{13,12},{... | collective-permute-start | bytes 983048 | tf_op jit(solution)/shard_map/ppermute | solution.py:15
  (48 other events, 146.4 us)
Sparse Core Ops, SparseCore 0:
  11.3 85.8 all-gather.1
  467.6 149.5 reduce-scatter.4
where the time goes:
time: 636 us; the launch traced here: 626 us
  waiting for transfers between devices  254 us (40%)
  matrix products  128 us (20%)
  local copies, waits for them, and re-layouts  126 us (20%)
  other arithmetic  80.1 us (13%)
  starting transfers between devices  22.5 us (4%)
  between operations  15.2 us (2%)
    unnamed x3, waiting for transfers between devices  146 us
    all_gather x1, waiting for transfers between devices, shards(): gathered = lax.all_gather(packed, 'dp', axis=1, tiled=True)[0]  84.3 us
    dot_general x19, matrix products, panel_product(): jnp.einsum('brc,bp->prc', products, placing, precision=lax.Precision.HIGH)  71.4 us
    dot_general x19, matrix products, panel_product(): jnp.einsum(form, picked, blocks, preferred_element_type=jnp.float32)  51.1 us
    gather x19, local copies, waits for them, and re-layouts, panel_product(): picked = jnp.take(panels, pick_index, axis=0)  49 us
    unnamed x20, other arithmetic  41 us
    unnamed x131, local copies, waits for them, and re-layouts  28.9 us
    ppermute x8, waiting for transfers between devices, from_behind(): return lax.ppermute(value, axis, pairs)  23.9 us
  transfers between devices with their start and end apart: 10, of which 8 were waited for; matrix products, arithmetic and copies ran while one was open for 11% of the time, Pallas kernels for 0%

commit v1 on v0

--- a/solution.py
+++ b/solution.py
@@ -143,7 +143,9 @@
         ],
         axis=2,
     )
-    gathered = lax.all_gather(packed, "dp", axis=1, tiled=True)[0]
+    gathered = jnp.concatenate(
+        lax.all_to_all(jnp.stack([packed] * lax.axis_size("dp")), "dp", 0, 0), axis=1
+    )[0]
     block_count = gathered.shape[0]
     up_blocks = gathered[:, :block_width].reshape(block_count, panel_width, panel_width)
     down_blocks = gathered[:, block_width : 2 * block_width].reshape(

time: 636 us -> 729 us (1.15)
  local copies, waits for them, and re-layouts: 126 us -> 168 us
  other arithmetic: 80.1 us -> 108 us
  starting transfers between devices: 22.5 us -> 35.4 us
  waiting for transfers between devices: 254 us -> 265 us
    all_to_all x0 -> x1, waiting for transfers between devices: none -> 94.7 us  [shards(): lax.all_to_all(jnp.stack([packed] * lax.axis_size('dp')), 'dp', 0, 0)]
    all_gather x1 -> x0, waiting for transfers between devices: 84.3 us -> none  [shards(): gathered = lax.all_gather(packed, 'dp', axis=1, tiled=True)[0]]
    unnamed x131 -> x141, local copies, waits for them, and re-layouts: 28.9 us -> 60.3 us
    another operation x0 -> x1, other arithmetic: none -> 27.2 us  [shards(): jnp.stack([packed] * lax.axis_size('dp'))]
    all_to_all x0 -> x1, starting transfers between devices: none -> 12.3 us  [shards(): lax.all_to_all(jnp.stack([packed] * lax.axis_size('dp')), 'dp', 0, 0)]
    unnamed x3 -> x2, waiting for transfers between devices: 146 us -> 147 us
  transfers between devices with their start and end apart: 10 -> 10, of which waited for: 8 -> 8; matrix products, arithmetic and copies ran while one was open for 11% -> 9% of each run, Pallas kernels for 0% -> 0%
where the time goes in v1:
time: 729 us; the launch traced here: 721 us
  waiting for transfers between devices  265 us (36%)
  local copies, waits for them, and re-layouts  168 us (23%)
  matrix products  130 us (18%)
  other arithmetic  108 us (15%)
  starting transfers between devices  35.4 us (5%)
  between operations  15.3 us (2%)
    unnamed x2, waiting for transfers between devices  147 us
    all_to_all x1, waiting for transfers between devices, shards(): lax.all_to_all(jnp.stack([packed] * lax.axis_size('dp')), 'dp', 0, 0)  94.7 us
    dot_general x19, matrix products, panel_product(): jnp.einsum('brc,bp->prc', products, placing, precision=lax.Precision.HIGH)  72.7 us
    unnamed x141, local copies, waits for them, and re-layouts  60.3 us
    dot_general x19, matrix products, panel_product(): jnp.einsum(form, picked, blocks, preferred_element_type=jnp.float32)  51.1 us
    gather x19, local copies, waits for them, and re-layouts, panel_product(): picked = jnp.take(panels, pick_index, axis=0)  49.5 us
    unnamed x20, other arithmetic  41 us
    another operation x1, other arithmetic, shards(): jnp.stack([packed] * lax.axis_size('dp'))  27.2 us
  transfers between devices with their start and end apart: 10, of which 8 were waited for; matrix products, arithmetic and copies ran while one was open for 9% of the time, Pallas kernels for 0%

profile of v1, /device:TPU:8, one launch (start us, length us, event | category | flops | bytes accessed | tf_op | source)
XLA Modules:
  0.0 721.0 jit_solution(3911748816636401525)
XLA Ops:
  9.8 5.6 stack.72
  15.9 27.2 %reduce.12 = bf16[64,32896]{1,0:T(8,128)(2,1)} reduce(bf16[64,1,1,32896]{3,2,1,0:T(2,128)(2,1)} %stack.72, bf16[]{:T(256)} %broadcast.595), dimensions={1,2}, to_apply=%stack.72.reduce_sub_computation | reduce | bytes 8421378 | tf_op jit(solution)/shard_map/stack | solution.py:147
  43.1 7.8 %reshape.843 = bf16[64,2,16448]{2,1,0:T(2,128)(2,1)} reshape(bf16[64,32896]{1,0:T(8,128)(2,1)} %reduce.12) | data formatting | bytes 8421376
  51.0 12.3 %all-to-all-start = ((bf16[64,2,16448]{2,1,0:T(2,128)(2,1)}), bf16[64,2,16448]{2,1,0:T(2,128)(2,1)}, u32[]{:S(2)}, u32[]{:S(2)}) async-start(bf16[64,2,16448]{2,1,0:T(2,128)(2,1)} %reshape.843), calls=%async_computation | async-start | bytes 8454144 | tf_op jit(solution)/shard_map/all_to_all | solution.py:147
  65.0 94.7 %all-to-all-done = bf16[64,2,16448]{2,1,0:T(2,128)(2,1)} async-done(((bf16[64,2,16448]{2,1,0:T(2,128)(2,1)}), bf16[64,2,16448]{2,1,0:T(2,128)(2,1)}, u32[]{:S(2)}, u32[]{:S(2)}) %all-to-all-start) | async-done | bytes 4210720 | tf_op jit(solution)/shard_map/all_to_all | solution.py:147
  159.7 24.5 %reshape.844 = bf16[64,1,1,32896]{3,2,1,0:T(2,128)(2,1)} reshape(bf16[64,2,16448]{2,1,0:T(2,128)(2,1)} %all-to-all-done) | data formatting | bytes 8421376
  184.2 3.8 copy.256
  216.3 7.1 collective-permute-done
  246.7 6.6 collective-permute-done.1
  275.2 3.9 collective-permute-start.2
  324.1 3.8 fusion.201
  327.9 6.7 bitcast_dynamic-update-slice_fusion.9
  375.6 3.8 fusion.198
  395.8 6.9 bitcast_dynamic-update-slice_fusion.8
  432.7 7.1 bitcast_dynamic-update-slice_fusion.7
  457.8 3.9 copy.114
  461.7 4.0 gather_fusion.20
  473.9 6.9 bitcast_dynamic-update-slice_fusion.6
  508.1 6.9 bitcast_dynamic-update-slice_fusion.5
  529.4 4.2 gather_fusion.19
  536.2 4.4 copy.258
  546.4 4.7 copy.257
  555.0 4.9 copy.143
  564.5 147.3 %reduce-scatter.5.cloned.1.call-done = f32[1,1,264,128]{3,2,1,0:T(8,128)} async-done(((f32[1,64,264,128]{3,2,1,0:T(8,128)}), f32[1,1,264,128]{3,2,1,0:T(8,128)}) %reduce-scatter.5.cloned.1.call-update) | async-done | bytes 135184
  (312 shorter events, 296.7 us)
Async XLA Ops:
  51.0 12.5 %copy-start.2 = (bf16[128,2560]{1,0:T(8,128)(2,1)S(1)}, bf16[128,2560]{1,0:T(8,128)(2,1)}, u32[]{:S(2)}) copy-start(bf16[128,2560]{1,0:T(8,128)(2,1)} %param.14) | copy-start | bytes 1966084
  51.0 12.7 %copy-start.50 = (s32[1,4,64]{2,1,0:T(4,128)S(1)}, s32[1,4,64]{2,1,0:T(4,128)}, u32[]{:S(2)}) copy-start(s32[1,4,64]{2,1,0:T(4,128)} %param.18) | copy-start | bytes 3076
  51.0 108.7 %all-to-all-start = ((bf16[64,2,16448]{2,1,0:T(2,128)(2,1)}), bf16[64,2,16448]{2,1,0:T(2,128)(2,1)}, u32[]{:S(2)}, u32[]{:S(2)}) async-start(bf16[64,2,16448]{2,1,0:T(2,128)(2,1)} %reshape.843), calls=%async_computation | async-start | bytes 8454144 | tf_op jit(solution)/shard_map/all_to_all | solution.py:147
  63.3 648.6 %reduce-scatter.5.cloned.1.call-start = ((), (), s32[]{:S(2)}) async-start(), calls=%async_computation.2 | async-start | bytes 8785920
  64.2 238.0 %copy-start.45 = (pred[64]{0:T(512)(128)(4,1)}, pred[64]{0:T(512)(128)(4,1)S(1)}, u32[]{:S(2)}) copy-start(pred[64]{0:T(512)(128)(4,1)S(1)} %get-tuple-element.60) | copy-start | bytes 196
  64.2 254.3 %copy-start.39 = (pred[64]{0:T(512)(128)(4,1)}, pred[64]{0:T(512)(128)(4,1)S(1)}, u32[]{:S(2)}) copy-start(pred[64]{0:T(512)(128)(4,1)S(1)} %get-tuple-element.62) | copy-start | bytes 196
  64.2 235.0 %copy-start.49 = (s32[1024]{0:T(1024)}, s32[1024]{0:T(1024)S(1)}, u32[]{:S(2)}) copy-start(s32[1024]{0:T(1024)S(1)} %get-tuple-element.91) | copy-start | bytes 12292
  64.2 252.6 %copy-start.47 = (s32[1024]{0:T(1024)}, s32[1024]{0:T(1024)S(1)}, u32[]{:S(2)}) copy-start(s32[1024]{0:T(1024)S(1)} %get-tuple-element.92) | copy-start | bytes 12292
  65.0 262.9 %copy-start.62 = (s32[64]{0:T(128)}, s32[64]{0:T(128)S(1)}, u32[]{:S(2)}) copy-start(s32[64]{0:T(128)S(1)} %get-tuple-element.59) | copy-start | bytes 772
  211.7 11.7 %collective-permute-start = (bf16[64,2560]{1,0:T(8,128)(2,1)S(1)}, bf16[64,2560]{1,0:T(8,128)(2,1)S(1)}, u32[]{:S(2)}, u32[]{:S(2)}) collective-permute-start(bf16[64,2560]{1,0:T(8,128)(2,1)S(1)} %fusion.309), channel_id=1, source_target_pairs={{0,1},{1,2},{2,3},{4,5},{5,6},{6,7},{8,9},{9,10},{10,11},{12,13},{... | collective-permute-start | bytes 983048 | tf_op jit(solution)/shard_map/ppermute | solution.py:15
  216.3 100.4 %copy-start.24 = (f32[2560]{0:T(1024)}, f32[2560]{0:T(1024)S(1)}, u32[]{:S(2)}) copy-start(f32[2560]{0:T(1024)S(1)} %reshape.568) | copy-start | bytes 30724
  239.6 6.2 copy-start.1
  242.1 11.2 %collective-permute-start.1 = (bf16[64,2560]{1,0:T(8,128)(2,1)}, bf16[64,2560]{1,0:T(8,128)(2,1)}, u32[]{:S(2)}, u32[]{:S(2)}) collective-permute-start(bf16[64,2560]{1,0:T(8,128)(2,1)} %fusion.282), channel_id=1, source_target_pairs={{0,1},{1,2},{2,3},{4,5},{5,6},{6,7},{8,9},{9,10},{10,11},{12,13},{... | collective-permute-start | bytes 983048 | tf_op jit(solution)/shard_map/ppermute | solution.py:15
  275.2 10.3 %collective-permute-start.2 = (bf16[64,2560]{1,0:T(8,128)(2,1)}, bf16[64,2560]{1,0:T(8,128)(2,1)}, u32[]{:S(2)}, u32[]{:S(2)}) collective-permute-start(bf16[64,2560]{1,0:T(8,128)(2,1)} %fusion.286), channel_id=1, source_target_pairs={{0,1},{1,2},{2,3},{4,5},{5,6},{6,7},{8,9},{9,10},{10,11},{12,13},{... | collective-permute-start | bytes 983048 | tf_op jit(solution)/shard_map/ppermute | solution.py:15
  279.7 11.8 %copy-start.48 = (s32[1024]{0:T(1024)}, s32[1024]{0:T(1024)S(1)}, u32[]{:S(2)}) copy-start(s32[1024]{0:T(1024)S(1)} %get-tuple-element.90) | copy-start | bytes 12292
  306.6 9.0 %collective-permute-start.3 = (bf16[64,2560]{1,0:T(8,128)(2,1)S(1)}, bf16[64,2560]{1,0:T(8,128)(2,1)S(1)}, u32[]{:S(2)}, u32[]{:S(2)}) collective-permute-start(bf16[64,2560]{1,0:T(8,128)(2,1)S(1)} %fusion.290), channel_id=1, source_target_pairs={{0,1},{1,2},{2,3},{4,5},{5,6},{6,7},{8,9},{9,10},{10,11},{12,13},{... | collective-permute-start | bytes 983048 | tf_op jit(solution)/shard_map/ppermute | solution.py:15
  354.6 33.2 %collective-permute-start.4 = (bf16[64,2560]{1,0:T(8,128)(2,1)}, bf16[64,2560]{1,0:T(8,128)(2,1)}, u32[]{:S(2)}, u32[]{:S(2)}) collective-permute-start(bf16[64,2560]{1,0:T(8,128)(2,1)} %fusion.276), channel_id=1, source_target_pairs={{1,0},{2,1},{3,2},{5,4},{6,5},{7,6},{9,8},{10,9},{11,10},{13,12},{... | collective-permute-start | bytes 983048 | tf_op jit(solution)/shard_map/ppermute | solution.py:15
  365.1 15.2 %copy-start.9 = (f32[64,20,128]{2,1,0:T(8,128)}, f32[64,20,128]{2,1,0:T(8,128)S(1)}, u32[]{:S(2)}) copy-start(f32[64,20,128]{2,1,0:T(8,128)S(1)} %reshape.573) | copy-start | bytes 1966084
  365.8 14.6 %copy-start.56 = (f32[64]{0:T(128)}, f32[64]{0:T(128)S(1)}, u32[]{:S(2)}) copy-start(f32[64]{0:T(128)S(1)} %add_rsqrt_fusion.3) | copy-start | bytes 772
  386.2 9.6 %copy-start.7 = (f32[64,20,128]{2,1,0:T(8,128)}, f32[64,20,128]{2,1,0:T(8,128)S(1)}, u32[]{:S(2)}) copy-start(f32[64,20,128]{2,1,0:T(8,128)S(1)} %reshape.575) | copy-start | bytes 1966084
  415.2 9.5 %collective-permute-start.5 = (bf16[64,2560]{1,0:T(8,128)(2,1)}, bf16[64,2560]{1,0:T(8,128)(2,1)}, u32[]{:S(2)}, u32[]{:S(2)}) collective-permute-start(bf16[64,2560]{1,0:T(8,128)(2,1)} %get-tuple-element.28), channel_id=1, source_target_pairs={{1,0},{2,1},{3,2},{5,4},{6,5},{7,6},{9,8},{10,9},{11,10},{13,12},{... | collective-permute-start | bytes 983048 | tf_op jit(solution)/shard_map/ppermute | solution.py:15
  421.7 11.0 %copy-start.5 = (f32[64,20,128]{2,1,0:T(8,128)}, f32[64,20,128]{2,1,0:T(8,128)S(1)}, u32[]{:S(2)}) copy-start(f32[64,20,128]{2,1,0:T(8,128)S(1)} %reshape.577) | copy-start | bytes 1966084
  452.3 15.2 %collective-permute-start.6 = (bf16[64,2560]{1,0:T(8,128)(2,1)}, bf16[64,2560]{1,0:T(8,128)(2,1)}, u32[]{:S(2)}, u32[]{:S(2)}) collective-permute-start(bf16[64,2560]{1,0:T(8,128)(2,1)} %get-tuple-element.26), channel_id=1, source_target_pairs={{1,0},{2,1},{3,2},{5,4},{6,5},{7,6},{9,8},{10,9},{11,10},{13,12},{... | collective-permute-start | bytes 983048 | tf_op jit(solution)/shard_map/ppermute | solution.py:15
  493.1 9.0 %collective-permute-start.7 = (bf16[64,2560]{1,0:T(8,128)(2,1)S(1)}, bf16[64,2560]{1,0:T(8,128)(2,1)S(1)}, u32[]{:S(2)}, u32[]{:S(2)}) collective-permute-start(bf16[64,2560]{1,0:T(8,128)(2,1)S(1)} %get-tuple-element.24), channel_id=1, source_target_pairs={{1,0},{2,1},{3,2},{5,4},{6,5},{7,6},{9,8},{10,9},{11,10},{13,12},{... | collective-permute-start | bytes 983048 | tf_op jit(solution)/shard_map/ppermute | solution.py:15
  (52 other events, 171.3 us)
Sparse Core Ops, SparseCore 0:
  560.0 151.7 reduce-scatter.4
